TPU v7x, 1024 devices: a whole 4x4x32 slice. The times are simulated.
1024 devices in a mesh: fsdp: 32 (over z), ty: 4 (over y_lo, core), tx: 8 (over y_hi, x).
Axes of the slice: x: 4, y: 4 (y_hi: 2, y_lo: 2; y = y_hi * 2 + y_lo), z: 32, core: 2. Of those that a mesh axis runs over, the one named last changes fastest.
Arguments:
- q_raw: bfloat16 [64, 32, 64, 1536], P('fsdp', 'ty', 'tx'), may hold values from -6 to 6
- k_raw: bfloat16 [64, 32, 64, 1536], P('fsdp', 'ty', 'tx'), may hold values from -6 to 6
- values: bfloat16 [64, 32, 64, 1536], P('fsdp', 'ty', 'tx'), may hold values from -6 to 6
- d_out: bfloat16 [64, 32, 64, 1536], P('fsdp', 'ty', 'tx'), may hold values from -6 to 6
- q_gain: float32 [128], P('fsdp'), may hold values from 0.1 to 1.9
- k_gain: float32 [128], P('fsdp'), may hold values from 0.1 to 1.9
- windows: int32 [12, 2], replicated, may hold values from 1 to 3, as said below
Outputs:
- out: bfloat16 [64, 32, 64, 1536], P('fsdp', 'ty', 'tx')
- q_grad: bfloat16 [64, 32, 64, 1536], P('fsdp', 'ty', 'tx')
- k_grad: bfloat16 [64, 32, 64, 1536], P('fsdp', 'ty', 'tx')
- v_grad: bfloat16 [64, 32, 64, 1536], P('fsdp', 'ty', 'tx')
- q_gain_grad: float32 [128], P('fsdp')
- k_gain_grad: float32 [128], P('fsdp')
Inputs may be any that keep to these rules, and one draw needn't show every extreme that they name: `windows`: every entry is 1 or 3; in each of the two columns some head has 3.
All inputs are finite; a program needn't handle non-finite values.
Results may differ from a plain program's by a relative error of at most 0.0083.
Values may be sent and summed in bfloat16 or wider, within the bound.
No kernel may reach another device: no remote copies, remote signals or barrier semaphores. Data moves between devices by JAX's collectives and lax.ppermute only.
A program may use at most 64 MiB of HBM per device.

v0:
```python
import math

import jax
import jax.numpy as jnp
from jax import lax
from jax.sharding import PartitionSpec as P

TILE = 8


NORM_EPS = 1e-06


def padded(cells, sides, width):
    for axis, dim in sides:
        count = lax.axis_size(axis)
        ends = count - 1
        head = lax.slice_in_dim(cells, 0, width, axis=dim)
        tail = lax.slice_in_dim(cells, cells.shape[dim] - width, cells.shape[dim], axis=dim)
        cells = jnp.concatenate(
            [
                lax.ppermute(tail, axis, [(i, (i + 1) % count) for i in range(ends)]),
                cells,
                lax.ppermute(head, axis, [((i + 1) % count, i) for i in range(ends)]),
            ],
            axis=dim,
        )
    return cells


def product(form, left, right):
    return jnp.einsum(form, left, right, preferred_element_type=jnp.float32)


def normalize(raw_field, norm_gain, head_count):
    floats = raw_field.astype(jnp.float32)
    floats = floats.reshape(floats.shape[:-1] + (head_count, norm_gain.shape[0]))
    inverse = lax.rsqrt(jnp.mean(floats * floats, axis=-1, keepdims=True) + NORM_EPS)
    normed = floats * inverse
    return (normed, inverse, (normed * norm_gain).astype(jnp.bfloat16))


def norm_backward(upstream, normed, inverse, norm_gain):
    gain_part = jnp.sum(upstream * normed, axis=tuple(range(upstream.ndim - 1)))
    scaled = upstream * norm_gain
    raw_grad = inverse * (scaled - normed * jnp.mean(scaled * normed, axis=-1, keepdims=True))
    return (raw_grad, gain_part)


def open_pairs(windows, tile_size):
    span = 3 * tile_size
    spots = jnp.arange(span * span, dtype=jnp.int32)
    step_rows = spots // span // tile_size - 1
    step_cols = spots % span // tile_size - 1
    tile_row = lax.axis_index("ty") + step_rows
    tile_col = lax.axis_index("tx") + step_cols
    inside = (
        (tile_row >= 0)
        & (tile_row < lax.axis_size("ty"))
        & (tile_col >= 0)
        & (tile_col < lax.axis_size("tx"))
    )
    reach_rows = ((windows[:, 0] - 1) // 2)[:, None]
    reach_cols = ((windows[:, 1] - 1) // 2)[:, None]
    within = (jnp.abs(step_rows)[None, :] <= reach_rows) & (
        jnp.abs(step_cols)[None, :] <= reach_cols
    )
    return inside[None, :] & within


def query_side(queries, keys_near, values_near, grad_out, open_mask, score_scale):
    scores = product("qhc,mhc->hqm", queries, keys_near) * score_scale
    weights = jnp.where(open_mask[:, None, :], jnp.exp(scores), 0.0)
    totals = jnp.sum(weights, axis=2)
    shares = weights / totals[:, :, None]
    shares_low = shares.astype(jnp.bfloat16)
    output = product("hqm,mhc->qhc", shares_low, values_near).astype(jnp.bfloat16)
    output_back = lax.optimization_barrier(output).astype(jnp.float32)
    row_delta = jnp.sum(grad_out.astype(jnp.float32) * output_back, axis=-1)
    share_grad = product("qhc,mhc->hqm", grad_out, values_near)
    score_grad = (shares * (share_grad - row_delta.T[:, :, None])).astype(jnp.bfloat16)
    query_grad = product("hqm,mhc->qhc", score_grad, keys_near) * score_scale
    return (output, totals.T, row_delta, query_grad)


def key_side(
    keys, value_rows, queries_near, grads_near, totals_near, delta_near, open_mask, score_scale
):
    scores = product("khc,mhc->hkm", keys, queries_near) * score_scale
    mask_rows = open_mask[:, None, :]
    weights = jnp.where(mask_rows, jnp.exp(scores), 0.0)
    divisor = jnp.where(open_mask, totals_near.T, 1.0)[:, None, :]
    shares = weights / divisor
    shares_low = shares.astype(jnp.bfloat16)
    value_grad = product("hkm,mhc->khc", shares_low, grads_near)
    share_grad = product("mhc,khc->hkm", grads_near, value_rows)
    score_grad = (shares * (share_grad - delta_near.T[:, None, :])).astype(jnp.bfloat16)
    key_grad = product("hkm,mhc->khc", score_grad, queries_near) * score_scale
    return (key_grad, value_grad)


def body(q_raw, k_raw, values, d_out, q_gain, k_gain, windows):
    head_count = windows.shape[0]
    q_gain_all, k_gain_all = (
        lax.all_gather(q_gain, "fsdp", axis=0, tiled=True),
        lax.all_gather(k_gain, "fsdp", axis=0, tiled=True),
    )
    frame_count, row_count, col_count, feature_count = q_raw.shape
    head_size = q_gain_all.shape[0]
    score_scale = 1.0 / math.sqrt(head_size)
    q_normed, q_inverse, q_hat = normalize(q_raw, q_gain_all, head_count)
    k_normed, k_inverse, k_hat = normalize(k_raw, k_gain_all, head_count)
    q_flat = q_hat.reshape(q_raw.shape)
    k_flat = k_hat.reshape(k_raw.shape)
    open_mask = open_pairs(windows, TILE)
    local_rows = row_count * col_count
    near_rows = (row_count + 2 * TILE) * (col_count + 2 * TILE)

    def as_local(field):
        return field.reshape(frame_count, local_rows, head_count, head_size)

    def as_near(field):
        return field.reshape(frame_count, near_rows, head_count, head_size)

    arrived = padded(jnp.stack([k_flat, values]), (("ty", 2), ("tx", 3)), TILE)

    def frame_query(queries, keys_near, values_near, grad_out):
        return query_side(queries, keys_near, values_near, grad_out, open_mask, score_scale)

    output, totals, row_delta, query_grad = jax.vmap(frame_query)(
        as_local(q_flat), as_near(arrived[0]), as_near(arrived[1]), as_local(d_out)
    )
    stat_grid = jnp.stack([totals, row_delta]).reshape(
        2, frame_count, row_count, col_count, head_count
    )
    row_sums = padded(stat_grid, (("ty", 2), ("tx", 3)), TILE)
    row_sums = row_sums.reshape(2, frame_count, near_rows, head_count)
    arrived_back = padded(jnp.stack([q_flat, d_out]), (("ty", 2), ("tx", 3)), TILE)
    query_fields = arrived_back[0]
    grad_fields = arrived_back[1]

    def frame_key(keys, value_rows, queries_near, grads_near, totals_near, delta_near):
        return key_side(
            keys,
            value_rows,
            queries_near,
            grads_near,
            totals_near,
            delta_near,
            open_mask,
            score_scale,
        )

    key_grad, value_grad = jax.vmap(frame_key)(
        as_local(k_flat),
        as_local(values),
        as_near(query_fields),
        as_near(grad_fields),
        row_sums[0],
        row_sums[1],
    )
    q_upstream = query_grad.reshape(q_normed.shape)
    k_upstream = key_grad.reshape(k_normed.shape)
    q_field_grad, q_part = norm_backward(q_upstream, q_normed, q_inverse, q_gain_all)
    k_field_grad, k_part = norm_backward(k_upstream, k_normed, k_inverse, k_gain_all)
    gain_parts = jnp.stack([q_part, k_part])
    whole_sum = lax.psum(gain_parts, ("fsdp", "ty", "tx"))
    share_len = whole_sum.shape[1] // lax.axis_size("fsdp")
    owned = lax.dynamic_slice_in_dim(whole_sum, lax.axis_index("fsdp") * share_len, share_len, 1)
    return (
        output.reshape(q_raw.shape),
        q_field_grad.reshape(q_raw.shape).astype(jnp.bfloat16),
        k_field_grad.reshape(k_raw.shape).astype(jnp.bfloat16),
        value_grad.reshape(values.shape).astype(jnp.bfloat16),
        owned[0],
        owned[1],
    )


def solution(mesh):
    return jax.shard_map(
        body,
        mesh=mesh,
        in_specs=(
            P("fsdp", "ty", "tx", None),
            P("fsdp", "ty", "tx", None),
            P("fsdp", "ty", "tx", None),
            P("fsdp", "ty", "tx", None),
            P("fsdp"),
            P("fsdp"),
            P(),
        ),
        out_specs=(
            P("fsdp", "ty", "tx", None),
            P("fsdp", "ty", "tx", None),
            P("fsdp", "ty", "tx", None),
            P("fsdp", "ty", "tx", None),
            P("fsdp"),
            P("fsdp"),
        ),
        check_vma=False,
    )
```

profile of v0, /device:TPU:6, one launch (start us, length us, event | category | flops | bytes accessed | tf_op | source)
XLA Modules:
  0.0 476.4 jit_solution(12158911140069214778)
XLA Ops:
  5.7 69.5 %all-reduce.2 = (f32[128]{0:T(128)S(1)}, f32[128]{0:T(128)S(1)}) all-reduce(f32[128]{0:T(128)S(1)} %dynamic-update-slice, f32[128]{0:T(128)S(1)} %dynamic-update-slice.1), channel_id=1, replica_groups=mesh['fsdp'=32,'ty'=4,'tx'=8] {'fsdp'}, use_global_device_ids=true, to_apply=%add | all-reduce | flops 256 | bytes 2048
  79.1 3.1 collective-permute-start
  84.0 2.7 pad_maximum_fusion.2
  86.7 2.7 collective-permute-start.3
  89.4 6.7 %collective-permute-start.2 = (bf16[2,2,24,8,1536]{4,3,2,1,0:T(8,128)(2,1)}, bf16[2,2,24,8,1536]{4,3,2,1,0:T(8,128)(2,1)}, u32[]{:S(2)}, u32[]{:S(2)}) collective-permute-start(bf16[2,2,24,8,1536]{4,3,2,1,0:T(8,128)(2,1)} %pad_maximum_fusion.2), channel_id=1, source_target_pairs={{0,1},{1,2},{2,3},{3,4},{4,5},{5,6},{6,7},{8,9},{9,10},{10,11},{11... | collective-permute-start | bytes 7077896 | tf_op jit(solution)/shard_map/ppermute | solution.py:22
  100.8 38.6 %collective-permute-done.3 = bf16[2,2,24,8,1536]{4,3,2,1,0:T(8,128)(2,1)} collective-permute-done((bf16[2,2,24,8,1536]{4,3,2,1,0:T(8,128)(2,1)}, bf16[2,2,24,8,1536]{4,3,2,1,0:T(8,128)(2,1)}, u32[]{:S(2)}, u32[]{:S(2)}) %collective-permute-start.3) | collective-permute-done | bytes 2359328 | tf_op jit(solution)/shard_map/ppermute | solution.py:24
  141.1 3.3 pad_maximum_fusion
  144.4 2.5 fusion.97
  146.8 7.4 %reshape_squeeze.12 = bf16[2,576,12,128]{3,2,1,0:T(8,128)(2,1)} reshape(bf16[1,2,24,24,1536]{4,3,2,1,0:T(8,128)(2,1)} %get-tuple-element.15) | data formatting | bytes 7077888 | tf_op jit(solution)/shard_map/reshape;squeeze | solution.py:123
  154.2 4.4 reshape_squeeze.13
  158.6 5.6 %fusion.3 = (f32[2,12,64]{2,1,0:T(8,128)S(1)}, f32[2,12,64,576]{3,2,1,0:T(8,128)S(1)}) fusion(pred[12,576]{1,0:T(8,128)(4,1)} %and_and_fusion, bf16[2,576,12,128]{3,2,1,0:T(8,128)(2,1)} %reshape_squeeze.13, f32[128]{0:T(128)} %copy-done.27, f32[2,64,12]{1,2,0:T(8,128)} %reshape.230, f32[2,64,12,128]{3,2,1,0:T(8,128)} %reshape.213), kind=kOutput, calls=%fused_computation.9 | convolution fusion | flops 229734912 | bytes 7884032 | tf_op jit(solution)/shard_map/vmap(qhc,mhc->hqm)/dot_general | solution.py:32
  164.3 2.7 fusion.51
  168.0 9.2 %multiply_reduce_fusion.1 = (f32[128]{0:T(128)}, f32[2,64,12]{1,2,0:T(8,128)S(1)}, f32[2,12,128,64]{2,3,1,0:T(8,128)S(1)}) fusion(f32[2,64,12]{1,2,0:T(8,128)S(1)} %copy-done.24, f32[2,64,12,128]{3,2,1,0:T(8,128)S(1)} %copy-done.19, f32[128]{0:T(128)S(1)} %copy-done.31, bf16[2,576,12,128]{3,2,1,0:T(8,128)(2,1)} %reshape_squeeze.13, ...), kind=kOutput, calls=%fused_computation.57 | convolution fusion | flops 459667840 | bytes 12615424 | tf_op jit(solution)/shard_map/vmap(hqm,mhc->qhc)/dot_general | solution.py:32
  181.0 9.7 %collective-permute-start.4 = (bf16[2,2,8,8,1536]{4,3,2,1,0:T(8,128)(2,1)S(1)}, bf16[2,2,8,8,1536]{4,3,2,1,0:T(8,128)(2,1)S(1)}, u32[]{:S(2)}, u32[]{:S(2)}) collective-permute-start(bf16[2,2,8,8,1536]{4,3,2,1,0:T(8,128)(2,1)S(1)} %pad_maximum_fusion.5), channel_id=1, source_target_pairs={{0,8},{8,16},{16,24},{1,9},{9,17},{17,25},{2,10},{10,18},{18,26},{... | collective-permute-start | bytes 2359304 | tf_op jit(solution)/shard_map/ppermute | solution.py:22
  196.1 7.7 %collective-permute-start.6 = (bf16[2,2,24,8,1536]{4,3,2,1,0:T(8,128)(2,1)}, bf16[2,2,24,8,1536]{4,3,2,1,0:T(8,128)(2,1)}, u32[]{:S(2)}, u32[]{:S(2)}) collective-permute-start(bf16[2,2,24,8,1536]{4,3,2,1,0:T(8,128)(2,1)} %pad_maximum_fusion.3), channel_id=1, source_target_pairs={{0,1},{1,2},{2,3},{3,4},{4,5},{5,6},{6,7},{8,9},{9,10},{10,11},{11... | collective-permute-start | bytes 7077896 | tf_op jit(solution)/shard_map/ppermute | solution.py:22
  206.7 11.7 %collective-permute-start.8 = (f32[2,2,8,8,12]{3,2,1,4,0:T(8,128)}, f32[2,2,8,8,12]{3,2,1,4,0:T(8,128)}, u32[]{:S(2)}, u32[]{:S(2)}) collective-permute-start(f32[2,2,8,8,12]{3,2,1,4,0:T(8,128)} %constant_dynamic-update-slice_fusion), channel_id=1, source_target_pairs={{0,8},{8,16},{16,24},{1,9},{9,17},{17,25},{2,10},{10,18},{18,26},{... | collective-permute-start | bytes 36872 | tf_op jit(solution)/shard_map/ppermute | solution.py:22
  226.7 7.5 %collective-permute-start.10 = (f32[2,2,24,8,12]{2,3,4,1,0:T(8,128)}, f32[2,2,24,8,12]{2,3,4,1,0:T(8,128)}, u32[]{:S(2)}, u32[]{:S(2)}) collective-permute-start(f32[2,2,24,8,12]{2,3,4,1,0:T(8,128)} %pad_maximum_fusion.7), channel_id=1, source_target_pairs={{0,1},{1,2},{2,3},{3,4},{4,5},{5,6},{6,7},{8,9},{9,10},{10,11},{11... | collective-permute-start | bytes 110600 | tf_op jit(solution)/shard_map/ppermute | solution.py:22
  241.1 9.5 %collective-permute-done.11 = f32[2,2,24,8,12]{2,3,4,1,0:T(8,128)} collective-permute-done((f32[2,2,24,8,12]{2,3,4,1,0:T(8,128)}, f32[2,2,24,8,12]{2,3,4,1,0:T(8,128)}, u32[]{:S(2)}, u32[]{:S(2)}) %collective-permute-start.11) | collective-permute-done | bytes 36896 | tf_op jit(solution)/shard_map/ppermute | solution.py:24
  257.4 3.3 pad_maximum_fusion.1
  263.1 7.4 %reshape_squeeze.14 = bf16[2,576,12,128]{3,2,1,0:T(8,128)(2,1)} reshape(bf16[1,2,24,24,1536]{4,3,2,1,0:T(8,128)(2,1)} %get-tuple-element.13) | data formatting | bytes 7077888 | tf_op jit(solution)/shard_map/reshape;squeeze | solution.py:123
  270.5 4.4 reshape_squeeze.15
  274.9 5.3 %select_divide_fusion = f32[2,12,64,576]{3,2,1,0:T(8,128)S(1)} fusion(f32[2,12,576]{2,1,0:T(8,128)} %copy.61, pred[12,576]{1,0:T(8,128)(4,1)} %and_and_fusion, bf16[2,576,12,128]{3,2,1,0:T(8,128)(2,1)} %reshape_squeeze.14, f32[128]{0:T(128)S(1)} %copy-done.26, f32[2,64,12,128]{3,2,1,0:T(8,128)} %reshape.217, f32[2,64,12]{1,2,0:T(8,128)} %reshape.232), kind=kOutput, calls=%fused_computation.6 | convolution fusion | flops 229736448 | bytes 7933184 | tf_op jit(solution)/shard_map/vmap(khc,mhc->hkm)/dot_general | solution.py:32
  282.9 8.9 %multiply_reduce_fusion = (f32[128]{0:T(128)S(1)}, f32[2,64,12]{1,2,0:T(8,128)S(1)}, f32[2,12,128,64]{2,3,1,0:T(8,128)S(1)}) fusion(f32[2,64,12]{1,2,0:T(8,128)S(1)} %copy-done.23, f32[2,64,12,128]{3,2,1,0:T(8,128)S(1)} %copy-done.18, f32[128]{0:T(128)S(1)} %copy-done.29, bf16[2,576,12,128]{3,2,1,0:T(8,128)(2,1)} %reshape_squeeze.14, ...), kind=kOutput, calls=%fused_computation.56 | convolution fusion | flops 457013632 | bytes 12651520 | tf_op jit(solution)/shard_map/vmap(hkm,mhc->khc)/dot_general | solution.py:32
  293.9 180.6 %psum.7 = f32[2,128]{1,0:T(2,128)S(1)} all-reduce(f32[2,128]{1,0:T(2,128)S(1)} %pad_maximum_fusion.8), channel_id=1, replica_groups=mesh['fsdp'=32,'ty'=4,'tx'=8] {'fsdp','ty','tx'}, use_global_device_ids=true, to_apply=%region_8.9 | all-reduce | flops 256 | bytes 2048 | tf_op jit(solution)/shard_map/psum | solution.py:167
  (151 shorter events, 60.1 us)
Async XLA Ops:
  0.6 95.5 %copy-start.9 = (bf16[2,8,8,1536]{3,2,1,0:T(8,128)(2,1)S(1)}, bf16[2,8,8,1536]{3,2,1,0:T(8,128)(2,1)}, u32[]{:S(2)}) copy-start(bf16[2,8,8,1536]{3,2,1,0:T(8,128)(2,1)} %param.7) | copy-start | bytes 1179652
  2.0 74.5 %copy-start.11 = (f32[2,8,8,12]{2,3,1,0:T(8,128)}, f32[2,8,8,12]{2,3,1,0:T(8,128)S(1)}, u32[]{:S(2)}) copy-start(f32[2,8,8,12]{2,3,1,0:T(8,128)S(1)} %add_rsqrt_fusion.1) | copy-start | bytes 18436
  75.2 24.3 %copy-start.25 = (f32[128]{0:T(128)}, f32[128]{0:T(128)S(1)}, u32[]{:S(2)}) copy-start(f32[128]{0:T(128)S(1)} %get-tuple-element.10) | copy-start | bytes 1540
  75.2 24.3 %copy-start.27 = (f32[128]{0:T(128)}, f32[128]{0:T(128)S(1)}, u32[]{:S(2)}) copy-start(f32[128]{0:T(128)S(1)} %get-tuple-element.11) | copy-start | bytes 1540
  77.6 22.5 %copy-start.28 = (s32[12,2]{0,1:T(2,128)S(1)}, s32[12,2]{0,1:T(2,128)}, u32[]{:S(2)}) copy-start(s32[12,2]{0,1:T(2,128)} %param.13) | copy-start | bytes 292
  77.6 63.5 %copy-start.1 = (bf16[2,8,8,1536]{3,2,1,0:T(8,128)(2,1)S(1)}, bf16[2,8,8,1536]{3,2,1,0:T(8,128)(2,1)}, u32[]{:S(2)}) copy-start(bf16[2,8,8,1536]{3,2,1,0:T(8,128)(2,1)} %param.9) | copy-start | bytes 1179652
  77.6 4.5 collective-permute-start.1
  79.1 4.9 %collective-permute-start = (bf16[2,2,8,8,1536]{4,3,2,1,0:T(8,128)(2,1)S(1)}, bf16[2,2,8,8,1536]{4,3,2,1,0:T(8,128)(2,1)S(1)}, u32[]{:S(2)}, u32[]{:S(2)}) collective-permute-start(bf16[2,2,8,8,1536]{4,3,2,1,0:T(8,128)(2,1)S(1)} %pad_maximum_fusion.4), channel_id=1, source_target_pairs={{0,8},{8,16},{16,24},{1,9},{9,17},{17,25},{2,10},{10,18},{18,26},{... | collective-permute-start | bytes 2359304 | tf_op jit(solution)/shard_map/ppermute | solution.py:22
  86.7 52.7 %collective-permute-start.3 = (bf16[2,2,24,8,1536]{4,3,2,1,0:T(8,128)(2,1)}, bf16[2,2,24,8,1536]{4,3,2,1,0:T(8,128)(2,1)}, u32[]{:S(2)}, u32[]{:S(2)}) collective-permute-start(bf16[2,2,24,8,1536]{4,3,2,1,0:T(8,128)(2,1)} %pad_maximum_fusion.2), channel_id=1, source_target_pairs={{1,0},{2,1},{3,2},{4,3},{5,4},{6,5},{7,6},{9,8},{10,9},{11,10},{12... | collective-permute-start | bytes 7077896 | tf_op jit(solution)/shard_map/ppermute | solution.py:24
  89.4 51.7 %collective-permute-start.2 = (bf16[2,2,24,8,1536]{4,3,2,1,0:T(8,128)(2,1)}, bf16[2,2,24,8,1536]{4,3,2,1,0:T(8,128)(2,1)}, u32[]{:S(2)}, u32[]{:S(2)}) collective-permute-start(bf16[2,2,24,8,1536]{4,3,2,1,0:T(8,128)(2,1)} %pad_maximum_fusion.2), channel_id=1, source_target_pairs={{0,1},{1,2},{2,3},{3,4},{4,5},{5,6},{6,7},{8,9},{9,10},{10,11},{11... | collective-permute-start | bytes 7077896 | tf_op jit(solution)/shard_map/ppermute | solution.py:22
  97.7 43.4 %copy-start.16 = (f32[2,8,8,12]{2,3,1,0:T(8,128)}, f32[2,8,8,12]{2,3,1,0:T(8,128)S(1)}, u32[]{:S(2)}) copy-start(f32[2,8,8,12]{2,3,1,0:T(8,128)S(1)} %add_rsqrt_fusion) | copy-start | bytes 18436
  179.5 54.7 %copy-start.12 = (f32[2,8,8,12]{2,3,1,0:T(8,128)S(1)}, f32[2,8,8,12]{2,3,1,0:T(8,128)}, u32[]{:S(2)}) copy-start(f32[2,8,8,12]{2,3,1,0:T(8,128)} %copy-done.11) | copy-start | bytes 18436
  179.6 55.4 %copy-start.5 = (bf16[2,8,8,1536]{3,2,1,0:T(8,128)(2,1)S(1)}, bf16[2,8,8,1536]{3,2,1,0:T(8,128)(2,1)}, u32[]{:S(2)}) copy-start(bf16[2,8,8,1536]{3,2,1,0:T(8,128)(2,1)} %param.8) | copy-start | bytes 1179652
  179.6 56.6 %copy-start.2 = (bf16[2,8,8,1536]{3,2,1,0:T(8,128)(2,1)S(1)}, bf16[2,8,8,1536]{3,2,1,0:T(8,128)(2,1)}, u32[]{:S(2)}) copy-start(bf16[2,8,8,1536]{3,2,1,0:T(8,128)(2,1)} %param.9) | copy-start | bytes 1179652
  179.6 11.1 %collective-permute-start.5 = (bf16[2,2,8,8,1536]{4,3,2,1,0:T(8,128)(2,1)S(1)}, bf16[2,2,8,8,1536]{4,3,2,1,0:T(8,128)(2,1)S(1)}, u32[]{:S(2)}, u32[]{:S(2)}) collective-permute-start(bf16[2,2,8,8,1536]{4,3,2,1,0:T(8,128)(2,1)S(1)} %pad_maximum_fusion.5), channel_id=1, source_target_pairs={{8,0},{16,8},{24,16},{9,1},{17,9},{25,17},{10,2},{18,10},{26,18},{... | collective-permute-start | bytes 2359304 | tf_op jit(solution)/shard_map/ppermute | solution.py:24
  181.0 11.5 %collective-permute-start.4 = (bf16[2,2,8,8,1536]{4,3,2,1,0:T(8,128)(2,1)S(1)}, bf16[2,2,8,8,1536]{4,3,2,1,0:T(8,128)(2,1)S(1)}, u32[]{:S(2)}, u32[]{:S(2)}) collective-permute-start(bf16[2,2,8,8,1536]{4,3,2,1,0:T(8,128)(2,1)S(1)} %pad_maximum_fusion.5), channel_id=1, source_target_pairs={{0,8},{8,16},{16,24},{1,9},{9,17},{17,25},{2,10},{10,18},{18,26},{... | collective-permute-start | bytes 2359304 | tf_op jit(solution)/shard_map/ppermute | solution.py:22
  194.2 63.1 %collective-permute-start.7 = (bf16[2,2,24,8,1536]{4,3,2,1,0:T(8,128)(2,1)}, bf16[2,2,24,8,1536]{4,3,2,1,0:T(8,128)(2,1)}, u32[]{:S(2)}, u32[]{:S(2)}) collective-permute-start(bf16[2,2,24,8,1536]{4,3,2,1,0:T(8,128)(2,1)} %pad_maximum_fusion.3), channel_id=1, source_target_pairs={{1,0},{2,1},{3,2},{4,3},{5,4},{6,5},{7,6},{9,8},{10,9},{11,10},{12... | collective-permute-start | bytes 7077896 | tf_op jit(solution)/shard_map/ppermute | solution.py:24
  196.1 61.2 %collective-permute-start.6 = (bf16[2,2,24,8,1536]{4,3,2,1,0:T(8,128)(2,1)}, bf16[2,2,24,8,1536]{4,3,2,1,0:T(8,128)(2,1)}, u32[]{:S(2)}, u32[]{:S(2)}) collective-permute-start(bf16[2,2,24,8,1536]{4,3,2,1,0:T(8,128)(2,1)} %pad_maximum_fusion.3), channel_id=1, source_target_pairs={{0,1},{1,2},{2,3},{3,4},{4,5},{5,6},{6,7},{8,9},{9,10},{10,11},{11... | collective-permute-start | bytes 7077896 | tf_op jit(solution)/shard_map/ppermute | solution.py:22
  205.4 14.0 %collective-permute-start.9 = (f32[2,2,8,8,12]{3,2,1,4,0:T(8,128)}, f32[2,2,8,8,12]{3,2,1,4,0:T(8,128)}, u32[]{:S(2)}, u32[]{:S(2)}) collective-permute-start(f32[2,2,8,8,12]{3,2,1,4,0:T(8,128)} %constant_dynamic-update-slice_fusion), channel_id=1, source_target_pairs={{8,0},{16,8},{24,16},{9,1},{17,9},{25,17},{10,2},{18,10},{26,18},{... | collective-permute-start | bytes 36872 | tf_op jit(solution)/shard_map/ppermute | solution.py:24
  206.7 14.5 %collective-permute-start.8 = (f32[2,2,8,8,12]{3,2,1,4,0:T(8,128)}, f32[2,2,8,8,12]{3,2,1,4,0:T(8,128)}, u32[]{:S(2)}, u32[]{:S(2)}) collective-permute-start(f32[2,2,8,8,12]{3,2,1,4,0:T(8,128)} %constant_dynamic-update-slice_fusion), channel_id=1, source_target_pairs={{0,8},{8,16},{16,24},{1,9},{9,17},{17,25},{2,10},{10,18},{18,26},{... | collective-permute-start | bytes 36872 | tf_op jit(solution)/shard_map/ppermute | solution.py:22
  224.8 25.8 %collective-permute-start.11 = (f32[2,2,24,8,12]{2,3,4,1,0:T(8,128)}, f32[2,2,24,8,12]{2,3,4,1,0:T(8,128)}, u32[]{:S(2)}, u32[]{:S(2)}) collective-permute-start(f32[2,2,24,8,12]{2,3,4,1,0:T(8,128)} %pad_maximum_fusion.7), channel_id=1, source_target_pairs={{1,0},{2,1},{3,2},{4,3},{5,4},{6,5},{7,6},{9,8},{10,9},{11,10},{12... | collective-permute-start | bytes 110600 | tf_op jit(solution)/shard_map/ppermute | solution.py:24
  226.7 25.6 %collective-permute-start.10 = (f32[2,2,24,8,12]{2,3,4,1,0:T(8,128)}, f32[2,2,24,8,12]{2,3,4,1,0:T(8,128)}, u32[]{:S(2)}, u32[]{:S(2)}) collective-permute-start(f32[2,2,24,8,12]{2,3,4,1,0:T(8,128)} %pad_maximum_fusion.7), channel_id=1, source_target_pairs={{0,1},{1,2},{2,3},{3,4},{4,5},{5,6},{6,7},{8,9},{9,10},{10,11},{11... | collective-permute-start | bytes 110600 | tf_op jit(solution)/shard_map/ppermute | solution.py:22
  291.8 183.4 %copy-start.6 = (bf16[2,8,8,1536]{3,2,1,0:T(8,128)(2,1)S(1)}, bf16[2,8,8,1536]{3,2,1,0:T(8,128)(2,1)}, u32[]{:S(2)}) copy-start(bf16[2,8,8,1536]{3,2,1,0:T(8,128)(2,1)} %param.8) | copy-start | bytes 1179652
  291.8 183.4 %copy-start.13 = (f32[2,8,8,12]{2,3,1,0:T(8,128)S(1)}, f32[2,8,8,12]{2,3,1,0:T(8,128)}, u32[]{:S(2)}) copy-start(f32[2,8,8,12]{2,3,1,0:T(8,128)} %copy-done.11) | copy-start | bytes 18436
  (21 other events, 80.8 us)
where the time goes:
time: 480 us; the launch traced here: 476 us
  blocking collectives  250 us (52%)
  starting transfers between devices  57.1 us (12%)
  local copies, waits for them, and re-layouts  56.1 us (12%)
  waiting for transfers between devices  55.2 us (12%)
  matrix products  33.4 us (7%)
  other arithmetic  22.4 us (5%)
    psum x1, blocking collectives, body(): whole_sum = lax.psum(gain_parts, ('fsdp', 'ty', 'tx'))  181 us
    unnamed x1, blocking collectives  69.5 us
    ppermute x6, waiting for transfers between devices, padded(): lax.ppermute(head, axis, [((i + 1) % count, i) for i in range(ends)])  48.1 us
    ppermute x6, starting transfers between devices, padded(): lax.ppermute(tail, axis, [(i, (i + 1) % count) for i in range(ends)])  46.4 us
    dot_general x6, matrix products, product(): return jnp.einsum(form, left, right, preferred_element_type=jnp.float32)  33.4 us
    another operation x4, local copies, waits for them, and re-layouts, as_near(): return field.reshape(frame_count, near_rows, head_count, head_size)  23.6 us
    concatenate x6, other arithmetic, padded(): jnp.concatenate([lax.ppermute(tail, axis, [(i, (i + 1) % count) for i in...  14.2 us
    ppermute x6, starting transfers between devices, padded(): lax.ppermute(head, axis, [((i + 1) % count, i) for i in range(ends)])  10.7 us
  transfers between devices with their start and end apart: 12, of which 6 were waited for; matrix products, arithmetic and copies ran while one was open for 5% of the time, Pallas kernels for 0%

commit v1 on v0

--- a/solution.py
+++ b/solution.py
@@ -28,6 +28,15 @@
     return cells
 
 
+def xor_sum(cells, axis):
+    count = lax.axis_size(axis)
+    step = 1
+    while step < count:
+        cells = cells + lax.ppermute(cells, axis, [(i, i ^ step) for i in range(count)])
+        step *= 2
+    return cells
+
+
 def product(form, left, right):
     return jnp.einsum(form, left, right, preferred_element_type=jnp.float32)
 
@@ -101,15 +110,23 @@
 
 def body(q_raw, k_raw, values, d_out, q_gain, k_gain, windows):
     head_count = windows.shape[0]
-    q_gain_all, k_gain_all = (
-        lax.all_gather(q_gain, "fsdp", axis=0, tiled=True),
-        lax.all_gather(k_gain, "fsdp", axis=0, tiled=True),
-    )
+    share_len = q_gain.shape[0]
+    head_size = share_len * lax.axis_size("fsdp")
+    gain_slots = jnp.zeros((2, head_size), jnp.float32)
+    gain_slots = lax.dynamic_update_slice_in_dim(
+        gain_slots, jnp.stack([q_gain, k_gain]), lax.axis_index("fsdp") * share_len, 1
+    )
+    gains = xor_sum(gain_slots, "fsdp")
+    q_gain_all, k_gain_all = gains[0], gains[1]
     frame_count, row_count, col_count, feature_count = q_raw.shape
-    head_size = q_gain_all.shape[0]
     score_scale = 1.0 / math.sqrt(head_size)
+    sides = (("ty", 2), ("tx", 3))
+    arrived = padded(jnp.stack([k_raw, values]), sides, TILE)
+    arrived_back = padded(jnp.stack([q_raw, d_out]), sides, TILE)
     q_normed, q_inverse, q_hat = normalize(q_raw, q_gain_all, head_count)
     k_normed, k_inverse, k_hat = normalize(k_raw, k_gain_all, head_count)
+    k_hat_near = normalize(arrived[0], k_gain_all, head_count)[2]
+    q_hat_near = normalize(arrived_back[0], q_gain_all, head_count)[2]
     q_flat = q_hat.reshape(q_raw.shape)
     k_flat = k_hat.reshape(k_raw.shape)
     open_mask = open_pairs(windows, TILE)
@@ -122,21 +139,18 @@
     def as_near(field):
         return field.reshape(frame_count, near_rows, head_count, head_size)
 
-    arrived = padded(jnp.stack([k_flat, values]), (("ty", 2), ("tx", 3)), TILE)
-
     def frame_query(queries, keys_near, values_near, grad_out):
         return query_side(queries, keys_near, values_near, grad_out, open_mask, score_scale)
 
     output, totals, row_delta, query_grad = jax.vmap(frame_query)(
-        as_local(q_flat), as_near(arrived[0]), as_near(arrived[1]), as_local(d_out)
+        as_local(q_flat), as_near(k_hat_near), as_near(arrived[1]), as_local(d_out)
     )
     stat_grid = jnp.stack([totals, row_delta]).reshape(
         2, frame_count, row_count, col_count, head_count
     )
     row_sums = padded(stat_grid, (("ty", 2), ("tx", 3)), TILE)
     row_sums = row_sums.reshape(2, frame_count, near_rows, head_count)
-    arrived_back = padded(jnp.stack([q_flat, d_out]), (("ty", 2), ("tx", 3)), TILE)
-    query_fields = arrived_back[0]
+    query_fields = q_hat_near
     grad_fields = arrived_back[1]
 
     def frame_key(keys, value_rows, queries_near, grads_near, totals_near, delta_near):
@@ -164,9 +178,10 @@
     q_field_grad, q_part = norm_backward(q_upstream, q_normed, q_inverse, q_gain_all)
     k_field_grad, k_part = norm_backward(k_upstream, k_normed, k_inverse, k_gain_all)
     gain_parts = jnp.stack([q_part, k_part])
-    whole_sum = lax.psum(gain_parts, ("fsdp", "ty", "tx"))
-    share_len = whole_sum.shape[1] // lax.axis_size("fsdp")
-    owned = lax.dynamic_slice_in_dim(whole_sum, lax.axis_index("fsdp") * share_len, share_len, 1)
+    plane_sum = xor_sum(xor_sum(gain_parts, "tx"), "ty")
+    owner_count = lax.axis_size("fsdp")
+    pieces = plane_sum.reshape(2, owner_count, share_len).transpose(1, 0, 2)
+    owned = lax.all_to_all(pieces, "fsdp", 0, 0, tiled=True).sum(axis=0)
     return (
         output.reshape(q_raw.shape),
         q_field_grad.reshape(q_raw.shape).astype(jnp.bfloat16),

time: 480 us -> 378 us (0.79)
  blocking collectives: 250 us -> 0 us
  starting transfers between devices: 57.1 us -> 125 us
  other arithmetic: 22.4 us -> 62 us
  local copies, waits for them, and re-layouts: 56.1 us -> 71.8 us
  waiting for transfers between devices: 55.2 us -> 67.9 us
  matrix products: 33.4 us -> 43.7 us
    psum x1 -> x0, blocking collectives: 181 us -> none  [body(): whole_sum = lax.psum(gain_parts, ('fsdp', 'ty', 'tx'))]
    unnamed x1 -> x0, blocking collectives: 69.5 us -> none
    ppermute x0 -> x10, starting transfers between devices: none -> 66.9 us  [xor_sum(): lax.ppermute(cells, axis, [(i, i ^ step) for i in range(count)])]
    convert_element_type x0 -> x2, local copies, waits for them, and re-layouts: none -> 18.1 us  [normalize(): floats = raw_field.astype(jnp.float32)]
    mul x0 -> x2, local copies, waits for them, and re-layouts: none -> 18.1 us  [normalize(): floats * floats]
    all_to_all x0 -> x1, waiting for transfers between devices: none -> 16.6 us  [body(): owned = lax.all_to_all(pieces, 'fsdp', 0, 0, tiled=True).sum(axis=0)]
    ppermute x0 -> x10, waiting for transfers between devices: none -> 16.4 us  [xor_sum(): lax.ppermute(cells, axis, [(i, i ^ step) for i in range(count)])]
    ppermute x6, waiting for transfers between devices: 48.1 us -> 33.8 us  [padded(): lax.ppermute(head, axis, [((i + 1) % count, i) for i in range(ends)])]
  transfers between devices with their start and end apart: 12 -> 23, of which waited for: 6 -> 11; matrix products, arithmetic and copies ran while one was open for 5% -> 17% of each run, Pallas kernels for 0% -> 0%
where the time goes in v1:
time: 378 us; the launch traced here: 372 us
  starting transfers between devices  125 us (33%)
  local copies, waits for them, and re-layouts  71.8 us (19%)
  waiting for transfers between devices  67.9 us (18%)
  other arithmetic  62 us (16%)
  matrix products  43.7 us (12%)
    ppermute x10, starting transfers between devices, xor_sum(): lax.ppermute(cells, axis, [(i, i ^ step) for i in range(count)])  66.9 us
    dot_general x6, matrix products, product(): return jnp.einsum(form, left, right, preferred_element_type=jnp.float32)  43.7 us
    ppermute x6, waiting for transfers between devices, padded(): lax.ppermute(head, axis, [((i + 1) % count, i) for i in range(ends)])  33.8 us
    ppermute x6, starting transfers between devices, padded(): lax.ppermute(tail, axis, [(i, (i + 1) % count) for i in range(ends)])  33.5 us
    convert_element_type x2, local copies, waits for them, and re-layouts, normalize(): floats = raw_field.astype(jnp.float32)  18.1 us
    mul x2, local copies, waits for them, and re-layouts, normalize(): floats * floats  18.1 us
    all_to_all x1, waiting for transfers between devices, body(): owned = lax.all_to_all(pieces, 'fsdp', 0, 0, tiled=True).sum(axis=0)  16.6 us
    ppermute x10, waiting for transfers between devices, xor_sum(): lax.ppermute(cells, axis, [(i, i ^ step) for i in range(count)])  16.4 us
  transfers between devices with their start and end apart: 23, of which 11 were waited for; matrix products, arithmetic and copies ran while one was open for 17% of the time, Pallas kernels for 0%

profile of v1, /device:TPU:6, one launch (start us, length us, event | category | flops | bytes accessed | tf_op | source)
XLA Modules:
  0.0 372.1 jit_solution(16921693135849450539)
XLA Ops:
  26.6 6.7 %collective-permute-start.2 = (bf16[2,2,24,8,1536]{4,3,2,1,0:T(8,128)(2,1)}, bf16[2,2,24,8,1536]{4,3,2,1,0:T(8,128)(2,1)}, u32[]{:S(2)}, u32[]{:S(2)}) collective-permute-start(bf16[2,2,24,8,1536]{4,3,2,1,0:T(8,128)(2,1)} %pad_maximum_fusion.2), channel_id=1, source_target_pairs={{0,1},{1,2},{2,3},{3,4},{4,5},{5,6},{6,7},{8,9},{9,10},{10,11},{11... | collective-permute-start | bytes 7077896 | tf_op jit(solution)/shard_map/ppermute | solution.py:22
  33.9 5.3 %collective-permute-start.5 = (f32[2,128]{1,0:T(2,128)S(1)}, f32[2,128]{1,0:T(2,128)S(1)}, u32[]{:S(2)}, u32[]{:S(2)}) collective-permute-start(f32[2,128]{1,0:T(2,128)S(1)} %add.162), channel_id=1, source_target_pairs={{0,64},{32,96},{64,0},{96,32},{128,192},{160,224},{192,128},{224,1... | collective-permute-start | bytes 3080 | tf_op jit(solution)/shard_map/ppermute | solution.py:35
  40.7 9.1 %collective-permute-start.6 = (f32[2,128]{1,0:T(2,128)S(1)}, f32[2,128]{1,0:T(2,128)S(1)}, u32[]{:S(2)}, u32[]{:S(2)}) collective-permute-start(f32[2,128]{1,0:T(2,128)S(1)} %add.163), channel_id=1, source_target_pairs={{0,128},{32,160},{64,192},{96,224},{128,0},{160,32},{192,64},{224,... | collective-permute-start | bytes 3080 | tf_op jit(solution)/shard_map/ppermute | solution.py:35
  51.3 15.7 %collective-permute-start.7 = (f32[2,128]{1,0:T(2,128)S(1)}, f32[2,128]{1,0:T(2,128)S(1)}, u32[]{:S(2)}, u32[]{:S(2)}) collective-permute-start(f32[2,128]{1,0:T(2,128)S(1)} %add.164), channel_id=1, source_target_pairs={{0,256},{32,288},{64,320},{96,352},{128,384},{160,416},{192,448},{... | collective-permute-start | bytes 3080 | tf_op jit(solution)/shard_map/ppermute | solution.py:35
  68.6 23.3 %collective-permute-start.8 = (f32[2,128]{1,0:T(2,128)S(1)}, f32[2,128]{1,0:T(2,128)S(1)}, u32[]{:S(2)}, u32[]{:S(2)}) collective-permute-start(f32[2,128]{1,0:T(2,128)S(1)} %add.165), channel_id=1, source_target_pairs={{0,512},{32,544},{64,576},{96,608},{128,640},{160,672},{192,704},{... | collective-permute-start | bytes 3080 | tf_op jit(solution)/shard_map/ppermute | solution.py:35
  104.0 8.0 %collective-permute-start.11 = (bf16[2,2,24,8,1536]{4,3,2,1,0:T(8,128)(2,1)S(1)}, bf16[2,2,24,8,1536]{4,3,2,1,0:T(8,128)(2,1)S(1)}, u32[]{:S(2)}, u32[]{:S(2)}) collective-permute-start(bf16[2,2,24,8,1536]{4,3,2,1,0:T(8,128)(2,1)S(1)} %pad_maximum_fusion.3), channel_id=1, source_target_pairs={{0,1},{1,2},{2,3},{3,4},{4,5},{5,6},{6,7},{8,9},{9,10},{10,11},{11... | collective-permute-start | bytes 7077896 | tf_op jit(solution)/shard_map/ppermute | solution.py:22
  124.7 33.7 %collective-permute-done.12 = bf16[2,2,24,8,1536]{4,3,2,1,0:T(8,128)(2,1)S(1)} collective-permute-done((bf16[2,2,24,8,1536]{4,3,2,1,0:T(8,128)(2,1)S(1)}, bf16[2,2,24,8,1536]{4,3,2,1,0:T(8,128)(2,1)S(1)}, u32[]{:S(2)}, u32[]{:S(2)}) %collective-permute-start.12) | collective-permute-done | bytes 2359328 | tf_op jit(solution)/shard_map/ppermute | solution.py:24
  169.1 9.1 %mul.265 = f32[2,24,24,12,128]{4,3,2,1,0:T(8,128)} reshape(f32[1,2,24,24,1536]{4,3,2,1,0:T(8,128)} %fusion.36) | data formatting | bytes 14155776 | tf_op jit(solution)/shard_map/mul | solution.py:47
  178.2 6.2 %reduce_sum.100 = f32[2,24,24,12]{3,2,1,0:T(8,128)S(1)} reduce(f32[2,24,24,12,128]{4,3,2,1,0:T(8,128)} %mul.265, f32[]{:T(128)} %constant.96.clone.1), dimensions={4}, to_apply=%region_1.0 | reduce | flops 1755648 | bytes 7133188 | tf_op jit(solution)/shard_map/reduce_sum | solution.py:47
  185.2 9.1 %reshape.254 = f32[2,576,12,128]{3,2,1,0:T(8,128)} reshape(f32[1,2,24,24,1536]{4,3,2,1,0:T(8,128)} %get-tuple-element.12) | data formatting | bytes 14155776 | tf_op jit(solution)/shard_map/convert_element_type | solution.py:45
  194.3 7.4 %reshape_squeeze.6 = bf16[2,576,12,128]{3,2,1,0:T(8,128)(2,1)} reshape(bf16[1,2,24,24,1536]{4,3,2,1,0:T(8,128)(2,1)} %get-tuple-element.13) | data formatting | bytes 7077888 | tf_op jit(solution)/shard_map/reshape;squeeze | solution.py:140
  201.7 9.0 %mul.298 = f32[2,24,24,12,128]{4,3,2,1,0:T(8,128)} reshape(f32[1,2,24,24,1536]{4,3,2,1,0:T(8,128)} %fusion.37) | data formatting | bytes 14155776 | tf_op jit(solution)/shard_map/mul | solution.py:47
  210.7 6.2 %reduce_sum.105 = f32[2,24,24,12]{3,2,1,0:T(8,128)S(1)} reduce(f32[2,24,24,12,128]{4,3,2,1,0:T(8,128)} %mul.298, f32[]{:T(128)} %constant.96.clone.1), dimensions={4}, to_apply=%region_6.7 | reduce | flops 1755648 | bytes 7133188 | tf_op jit(solution)/shard_map/reduce_sum | solution.py:47
  217.7 9.0 %reshape.255 = f32[2,576,12,128]{3,2,1,0:T(8,128)} reshape(f32[1,2,24,24,1536]{4,3,2,1,0:T(8,128)} %get-tuple-element.11) | data formatting | bytes 14155776 | tf_op jit(solution)/shard_map/convert_element_type | solution.py:45
  226.7 9.9 %multiply_convert_fusion = (bf16[2,576,12,128]{3,2,1,0:T(8,128)(2,1)}, bf16[2,576,12,128]{3,2,1,0:T(8,128)(2,1)S(1)}) fusion(f32[2,576,12,128]{3,2,1,0:T(8,128)} %reshape.255, f32[128]{0:T(128)S(1)} %get-tuple-element.22, f32[2,576,12]{2,1,0:T(8,128)S(1)} %bitcast.157, f32[128]{0:T(128)S(1)} %get-tuple-element.23, f32[2,576,12,128]{3,2,1,0:T(8,128)} %reshape.254, ...), kind=kLoop, calls=%fused_computation | loop fusion | flops 10616832 | bytes 21345280 | tf_op jit(solution)/shard_map/convert_element_type | solution.py:49
  241.3 5.8 %fusion.53 = bf16[2,64,12,128]{3,1,2,0:T(8,128)(2,1)S(1)} fusion(bf16[2,576,12,128]{3,2,1,0:T(8,128)(2,1)} %reshape_squeeze.6, f32[2,12,64,576]{3,2,1,0:T(8,128)} %get-tuple-element.25, f32[2,12,64]{2,1,0:T(8,128)S(1)} %get-tuple-element.24, pred[12,576]{1,0:T(8,128)(4,1)S(1)} %and_and_fusion), kind=kOutput, calls=%fused_computation.41 | convolution fusion | flops 230227968 | bytes 7484160 | tf_op jit(solution)/shard_map/vmap(hqm,mhc->qhc)/dot_general | solution.py:41
  252.6 11.1 %multiply_reduce_fusion.1 = (f32[128]{0:T(128)}, f32[2,64,12]{1,2,0:T(8,128)}, f32[2,12,128,64]{2,3,1,0:T(8,128)}) fusion(f32[2,64,12]{1,2,0:T(8,128)S(1)} %reshape.256, f32[2,64,12,128]{3,2,1,0:T(8,128)S(1)} %copy-done.8, f32[128]{0:T(128)S(1)} %get-tuple-element.19, bf16[2,576,12,128]{3,2,1,0:T(8,128)(2,1)} %copy-done.4, f32[2,12,64]{2,1,0:T(8,128)S(1)} %bitcast.160, ...), kind=kOutput, calls=%fused_computation.63 | convolution fusion | flops 459667840 | bytes 12615424 | tf_op jit(solution)/shard_map/vmap(hqm,mhc->qhc)/dot_general | solution.py:41
  267.1 8.0 %collective-permute-start.15 = (f32[2,2,24,8,12]{2,3,4,1,0:T(8,128)S(1)}, f32[2,2,24,8,12]{2,3,4,1,0:T(8,128)}, u32[]{:S(2)}, u32[]{:S(2)}) collective-permute-start(f32[2,2,24,8,12]{2,3,4,1,0:T(8,128)S(1)} %pad_maximum_fusion.7), channel_id=1, source_target_pairs={{0,1},{1,2},{2,3},{3,4},{4,5},{5,6},{6,7},{8,9},{9,10},{10,11},{11... | collective-permute-start | bytes 110600 | tf_op jit(solution)/shard_map/ppermute | solution.py:22
  276.3 7.6 %reshape_squeeze.7 = bf16[2,576,12,128]{3,2,1,0:T(8,128)(2,1)} reshape(bf16[1,2,24,24,1536]{4,3,2,1,0:T(8,128)(2,1)} %get-tuple-element.10) | data formatting | bytes 7077888 | tf_op jit(solution)/shard_map/reshape;squeeze | solution.py:140
  288.3 7.2 %select_divide_fusion = f32[2,12,64,576]{3,2,1,0:T(8,128)} fusion(f32[2,12,576]{2,1,0:T(8,128)S(1)} %copy.110, pred[12,576]{1,0:T(8,128)(4,1)} %copy-done.10, bf16[2,576,12,128]{3,2,1,0:T(8,128)(2,1)} %get-tuple-element.30, f32[128]{0:T(128)} %copy-done.16, f32[2,64,12,128]{3,2,1,0:T(8,128)} %reshape.250, f32[2,64,12]{1,2,0:T(8,128)} %reshape.260), kind=kOutput, calls=%fused_computation.8 | convolution fusion | flops 229736448 | bytes 7933184 | tf_op jit(solution)/shard_map/vmap(khc,mhc->hkm)/dot_general | solution.py:41
  295.5 9.9 %multiply_reduce_fusion = (f32[128]{0:T(128)S(1)}, f32[2,64,12]{1,2,0:T(8,128)S(1)}, f32[2,12,128,64]{2,3,1,0:T(8,128)}) fusion(f32[2,64,12]{1,2,0:T(8,128)S(1)} %copy-done.14, f32[2,64,12,128]{3,2,1,0:T(8,128)S(1)} %copy-done.6, f32[128]{0:T(128)S(1)} %copy-done.21, bf16[2,576,12,128]{3,2,1,0:T(8,128)(2,1)} %get-tuple-element.30, ...), kind=kOutput, calls=%fused_computation.62 | convolution fusion | flops 457013632 | bytes 12651520 | tf_op jit(solution)/shard_map/vmap(hkm,mhc->khc)/dot_general | solution.py:41
  334.2 14.0 %all-to-all-start = ((f32[32,2,4]{2,1,0:T(2,128)}), f32[32,2,4]{2,1,0:T(2,128)S(1)}, u32[]{:S(2)}, u32[]{:S(2)}) async-start(f32[32,2,4]{2,1,0:T(2,128)} %copy.121), calls=%async_computation | async-start | bytes 65536 | tf_op jit(solution)/shard_map/all_to_all | solution.py:184
  348.2 5.2 %fusion.48 = bf16[2,64,12,128]{3,1,2,0:T(8,128)(2,1)S(1)} fusion(bf16[2,576,12,128]{3,2,1,0:T(8,128)(2,1)} %reshape_squeeze.7, f32[2,12,64,576]{3,2,1,0:T(8,128)} %select_divide_fusion), kind=kOutput, calls=%fused_computation.40 | convolution fusion | flops 227573760 | bytes 7471104 | tf_op jit(solution)/shard_map/vmap(hkm,mhc->khc)/dot_general | solution.py:41
  354.7 16.6 %all-to-all-done = f32[32,2,4]{2,1,0:T(2,128)S(1)} async-done(((f32[32,2,4]{2,1,0:T(2,128)}), f32[32,2,4]{2,1,0:T(2,128)S(1)}, u32[]{:S(2)}, u32[]{:S(2)}) %all-to-all-start) | async-done | bytes 1056 | tf_op jit(solution)/shard_map/all_to_all | solution.py:184
  (173 shorter events, 117.1 us)
Async XLA Ops:
  2.8 17.9 %collective-permute-start.1 = (bf16[2,2,8,8,1536]{4,3,2,1,0:T(8,128)(2,1)}, bf16[2,2,8,8,1536]{4,3,2,1,0:T(8,128)(2,1)}, u32[]{:S(2)}, u32[]{:S(2)}) collective-permute-start(bf16[2,2,8,8,1536]{4,3,2,1,0:T(8,128)(2,1)} %pad_maximum_fusion.4), channel_id=1, source_target_pairs={{8,0},{16,8},{24,16},{9,1},{17,9},{25,17},{10,2},{18,10},{26,18},{... | collective-permute-start | bytes 2359304 | tf_op jit(solution)/shard_map/ppermute | solution.py:24
  4.1 16.6 %collective-permute-start = (bf16[2,2,8,8,1536]{4,3,2,1,0:T(8,128)(2,1)}, bf16[2,2,8,8,1536]{4,3,2,1,0:T(8,128)(2,1)}, u32[]{:S(2)}, u32[]{:S(2)}) collective-permute-start(bf16[2,2,8,8,1536]{4,3,2,1,0:T(8,128)(2,1)} %pad_maximum_fusion.4), channel_id=1, source_target_pairs={{0,8},{8,16},{16,24},{1,9},{9,17},{17,25},{2,10},{10,18},{18,26},{... | collective-permute-start | bytes 2359304 | tf_op jit(solution)/shard_map/ppermute | solution.py:22
  10.3 91.5 %collective-permute-start.10 = (bf16[2,2,8,8,1536]{4,3,2,1,0:T(8,128)(2,1)}, bf16[2,2,8,8,1536]{4,3,2,1,0:T(8,128)(2,1)S(1)}, u32[]{:S(2)}, u32[]{:S(2)}) collective-permute-start(bf16[2,2,8,8,1536]{4,3,2,1,0:T(8,128)(2,1)} %pad_maximum_fusion.5), channel_id=1, source_target_pairs={{8,0},{16,8},{24,16},{9,1},{17,9},{25,17},{10,2},{18,10},{26,18},{... | collective-permute-start | bytes 2359304 | tf_op jit(solution)/shard_map/ppermute | solution.py:24
  11.6 90.2 %collective-permute-start.9 = (bf16[2,2,8,8,1536]{4,3,2,1,0:T(8,128)(2,1)}, bf16[2,2,8,8,1536]{4,3,2,1,0:T(8,128)(2,1)S(1)}, u32[]{:S(2)}, u32[]{:S(2)}) collective-permute-start(bf16[2,2,8,8,1536]{4,3,2,1,0:T(8,128)(2,1)} %pad_maximum_fusion.5), channel_id=1, source_target_pairs={{0,8},{8,16},{16,24},{1,9},{9,17},{17,25},{2,10},{10,18},{18,26},{... | collective-permute-start | bytes 2359304 | tf_op jit(solution)/shard_map/ppermute | solution.py:22
  15.5 18.2 %collective-permute-start.4 = (f32[2,128]{1,0:T(2,128)S(1)}, f32[2,128]{1,0:T(2,128)S(1)}, u32[]{:S(2)}, u32[]{:S(2)}) collective-permute-start(f32[2,128]{1,0:T(2,128)S(1)} %dynamic_update_slice.5), channel_id=1, source_target_pairs={{0,32},{32,0},{64,96},{96,64},{128,160},{160,128},{192,224},{224,1... | collective-permute-start | bytes 3080 | tf_op jit(solution)/shard_map/ppermute | solution.py:35
  23.9 88.1 %collective-permute-start.3 = (bf16[2,2,24,8,1536]{4,3,2,1,0:T(8,128)(2,1)}, bf16[2,2,24,8,1536]{4,3,2,1,0:T(8,128)(2,1)}, u32[]{:S(2)}, u32[]{:S(2)}) collective-permute-start(bf16[2,2,24,8,1536]{4,3,2,1,0:T(8,128)(2,1)} %pad_maximum_fusion.2), channel_id=1, source_target_pairs={{1,0},{2,1},{3,2},{4,3},{5,4},{6,5},{7,6},{9,8},{10,9},{11,10},{12... | collective-permute-start | bytes 7077896 | tf_op jit(solution)/shard_map/ppermute | solution.py:24
  26.6 85.4 %collective-permute-start.2 = (bf16[2,2,24,8,1536]{4,3,2,1,0:T(8,128)(2,1)}, bf16[2,2,24,8,1536]{4,3,2,1,0:T(8,128)(2,1)}, u32[]{:S(2)}, u32[]{:S(2)}) collective-permute-start(bf16[2,2,24,8,1536]{4,3,2,1,0:T(8,128)(2,1)} %pad_maximum_fusion.2), channel_id=1, source_target_pairs={{0,1},{1,2},{2,3},{3,4},{4,5},{5,6},{6,7},{8,9},{9,10},{10,11},{11... | collective-permute-start | bytes 7077896 | tf_op jit(solution)/shard_map/ppermute | solution.py:22
  33.9 6.8 %collective-permute-start.5 = (f32[2,128]{1,0:T(2,128)S(1)}, f32[2,128]{1,0:T(2,128)S(1)}, u32[]{:S(2)}, u32[]{:S(2)}) collective-permute-start(f32[2,128]{1,0:T(2,128)S(1)} %add.162), channel_id=1, source_target_pairs={{0,64},{32,96},{64,0},{96,32},{128,192},{160,224},{192,128},{224,1... | collective-permute-start | bytes 3080 | tf_op jit(solution)/shard_map/ppermute | solution.py:35
  40.7 10.6 %collective-permute-start.6 = (f32[2,128]{1,0:T(2,128)S(1)}, f32[2,128]{1,0:T(2,128)S(1)}, u32[]{:S(2)}, u32[]{:S(2)}) collective-permute-start(f32[2,128]{1,0:T(2,128)S(1)} %add.163), channel_id=1, source_target_pairs={{0,128},{32,160},{64,192},{96,224},{128,0},{160,32},{192,64},{224,... | collective-permute-start | bytes 3080 | tf_op jit(solution)/shard_map/ppermute | solution.py:35
  51.3 17.3 %collective-permute-start.7 = (f32[2,128]{1,0:T(2,128)S(1)}, f32[2,128]{1,0:T(2,128)S(1)}, u32[]{:S(2)}, u32[]{:S(2)}) collective-permute-start(f32[2,128]{1,0:T(2,128)S(1)} %add.164), channel_id=1, source_target_pairs={{0,256},{32,288},{64,320},{96,352},{128,384},{160,416},{192,448},{... | collective-permute-start | bytes 3080 | tf_op jit(solution)/shard_map/ppermute | solution.py:35
  68.6 32.0 %collective-permute-start.8 = (f32[2,128]{1,0:T(2,128)S(1)}, f32[2,128]{1,0:T(2,128)S(1)}, u32[]{:S(2)}, u32[]{:S(2)}) collective-permute-start(f32[2,128]{1,0:T(2,128)S(1)} %add.165), channel_id=1, source_target_pairs={{0,512},{32,544},{64,576},{96,608},{128,640},{160,672},{192,704},{... | collective-permute-start | bytes 3080 | tf_op jit(solution)/shard_map/ppermute | solution.py:35
  92.0 160.6 %copy-start.10 = (pred[12,576]{1,0:T(8,128)(4,1)}, pred[12,576]{1,0:T(8,128)(4,1)S(1)}, u32[]{:S(2)}) copy-start(pred[12,576]{1,0:T(8,128)(4,1)S(1)} %and_and_fusion) | copy-start | bytes 20740
  102.0 56.4 %collective-permute-start.12 = (bf16[2,2,24,8,1536]{4,3,2,1,0:T(8,128)(2,1)S(1)}, bf16[2,2,24,8,1536]{4,3,2,1,0:T(8,128)(2,1)S(1)}, u32[]{:S(2)}, u32[]{:S(2)}) collective-permute-start(bf16[2,2,24,8,1536]{4,3,2,1,0:T(8,128)(2,1)S(1)} %pad_maximum_fusion.3), channel_id=1, source_target_pairs={{1,0},{2,1},{3,2},{4,3},{5,4},{6,5},{7,6},{9,8},{10,9},{11,10},{12... | collective-permute-start | bytes 7077896 | tf_op jit(solution)/shard_map/ppermute | solution.py:24
  104.0 55.6 %collective-permute-start.11 = (bf16[2,2,24,8,1536]{4,3,2,1,0:T(8,128)(2,1)S(1)}, bf16[2,2,24,8,1536]{4,3,2,1,0:T(8,128)(2,1)S(1)}, u32[]{:S(2)}, u32[]{:S(2)}) collective-permute-start(bf16[2,2,24,8,1536]{4,3,2,1,0:T(8,128)(2,1)S(1)} %pad_maximum_fusion.3), channel_id=1, source_target_pairs={{0,1},{1,2},{2,3},{3,4},{4,5},{5,6},{6,7},{8,9},{9,10},{10,11},{11... | collective-permute-start | bytes 7077896 | tf_op jit(solution)/shard_map/ppermute | solution.py:22
  247.6 16.2 %collective-permute-start.14 = (f32[2,2,8,8,12]{3,2,1,4,0:T(8,128)S(1)}, f32[2,2,8,8,12]{3,2,1,4,0:T(8,128)S(1)}, u32[]{:S(2)}, u32[]{:S(2)}) collective-permute-start(f32[2,2,8,8,12]{3,2,1,4,0:T(8,128)S(1)} %constant_dynamic-update-slice_fusion), channel_id=1, source_target_pairs={{8,0},{16,8},{24,16},{9,1},{17,9},{25,17},{10,2},{18,10},{26,18},{... | collective-permute-start | bytes 36872 | tf_op jit(solution)/shard_map/ppermute | solution.py:24
  248.9 15.1 %collective-permute-start.13 = (f32[2,2,8,8,12]{3,2,1,4,0:T(8,128)S(1)}, f32[2,2,8,8,12]{3,2,1,4,0:T(8,128)}, u32[]{:S(2)}, u32[]{:S(2)}) collective-permute-start(f32[2,2,8,8,12]{3,2,1,4,0:T(8,128)S(1)} %constant_dynamic-update-slice_fusion), channel_id=1, source_target_pairs={{0,8},{8,16},{16,24},{1,9},{9,17},{17,25},{2,10},{10,18},{18,26},{... | collective-permute-start | bytes 36872 | tf_op jit(solution)/shard_map/ppermute | solution.py:22
  265.2 18.8 %collective-permute-start.16 = (f32[2,2,24,8,12]{2,3,4,1,0:T(8,128)S(1)}, f32[2,2,24,8,12]{2,3,4,1,0:T(8,128)S(1)}, u32[]{:S(2)}, u32[]{:S(2)}) collective-permute-start(f32[2,2,24,8,12]{2,3,4,1,0:T(8,128)S(1)} %pad_maximum_fusion.7), channel_id=1, source_target_pairs={{1,0},{2,1},{3,2},{4,3},{5,4},{6,5},{7,6},{9,8},{10,9},{11,10},{12... | collective-permute-start | bytes 110600 | tf_op jit(solution)/shard_map/ppermute | solution.py:24
  267.1 17.5 %collective-permute-start.15 = (f32[2,2,24,8,12]{2,3,4,1,0:T(8,128)S(1)}, f32[2,2,24,8,12]{2,3,4,1,0:T(8,128)}, u32[]{:S(2)}, u32[]{:S(2)}) collective-permute-start(f32[2,2,24,8,12]{2,3,4,1,0:T(8,128)S(1)} %pad_maximum_fusion.7), channel_id=1, source_target_pairs={{0,1},{1,2},{2,3},{3,4},{4,5},{5,6},{6,7},{8,9},{9,10},{10,11},{11... | collective-permute-start | bytes 110600 | tf_op jit(solution)/shard_map/ppermute | solution.py:22
  305.5 5.5 %collective-permute-start.17 = (f32[2,128]{1,0:T(2,128)S(1)}, f32[2,128]{1,0:T(2,128)S(1)}, u32[]{:S(2)}, u32[]{:S(2)}) collective-permute-start(f32[2,128]{1,0:T(2,128)S(1)} %pad_maximum_fusion.9), channel_id=1, source_target_pairs={{0,1},{1,0},{2,3},{3,2},{4,5},{5,4},{6,7},{7,6},{8,9},{9,8},{10,11... | collective-permute-start | bytes 3080 | tf_op jit(solution)/shard_map/ppermute | solution.py:35
  311.0 7.0 %collective-permute-start.18 = (f32[2,128]{1,0:T(2,128)S(1)}, f32[2,128]{1,0:T(2,128)S(1)}, u32[]{:S(2)}, u32[]{:S(2)}) collective-permute-start(f32[2,128]{1,0:T(2,128)S(1)} %fusion.98), channel_id=1, source_target_pairs={{0,2},{1,3},{2,0},{3,1},{4,6},{5,7},{6,4},{7,5},{8,10},{9,11},{10,... | collective-permute-start | bytes 3080 | tf_op jit(solution)/shard_map/ppermute | solution.py:35
  317.9 7.0 %collective-permute-start.19 = (f32[2,128]{1,0:T(2,128)S(1)}, f32[2,128]{1,0:T(2,128)S(1)}, u32[]{:S(2)}, u32[]{:S(2)}) collective-permute-start(f32[2,128]{1,0:T(2,128)S(1)} %fusion.109), channel_id=1, source_target_pairs={{0,4},{1,5},{2,6},{3,7},{4,0},{5,1},{6,2},{7,3},{8,12},{9,13},{10,... | collective-permute-start | bytes 3080 | tf_op jit(solution)/shard_map/ppermute | solution.py:35
  324.9 3.0 collective-permute-start.20
  328.0 5.5 %collective-permute-start.21 = (f32[2,128]{1,0:T(2,128)S(1)}, f32[2,128]{1,0:T(2,128)S(1)}, u32[]{:S(2)}, u32[]{:S(2)}) collective-permute-start(f32[2,128]{1,0:T(2,128)S(1)} %add.173), channel_id=1, source_target_pairs={{0,16},{8,24},{16,0},{24,8},{1,17},{9,25},{17,1},{25,9},{2,18},{10... | collective-permute-start | bytes 3080 | tf_op jit(solution)/shard_map/ppermute | solution.py:35
  334.2 37.1 %all-to-all-start = ((f32[32,2,4]{2,1,0:T(2,128)}), f32[32,2,4]{2,1,0:T(2,128)S(1)}, u32[]{:S(2)}, u32[]{:S(2)}) async-start(f32[32,2,4]{2,1,0:T(2,128)} %copy.121), calls=%async_computation | async-start | bytes 65536 | tf_op jit(solution)/shard_map/all_to_all | solution.py:184
  (21 other events, 508.8 us)
